TPU v7x, 32 devices: a whole 2x2x4 slice. The times are simulated.
32 devices in a mesh: member: 2 (over x), row: 16 (over z, y, core).
Axes of the slice: x: 2, y: 2, z: 4, core: 2. Of those that a mesh axis runs over, the one named last changes fastest.
Arguments:
- coarse: bfloat16 [384, 128, 128], P('row', 'member'), parts along dimension 1, may hold values from -6 to 6
- skip_field: bfloat16 [192, 256, 256], P(None, ('member', 'row')), parts along dimension 1, may hold values from -6 to 6
- up_weight: bfloat16 [4, 4, 384, 192], replicated, may hold values from -0.15625 to 0.15625
- up_bias: float32 [192], replicated, may hold values from -3 to 3
- conv_weight: bfloat16 [3, 3, 384, 192], replicated, may hold values from -0.109375 to 0.109375
- conv_bias: float32 [192], replicated, may hold values from -3 to 3
Outputs:
- decoded: bfloat16 [192, 256, 256], P(None, ('member', 'row')), parts along dimension 1
There are 2 independent parts, one for each index of `member`. A program takes and returns all parts, laid end to end along the dimension named above; an argument that names none is the same for every part. Nothing has to cross between parts.
All inputs are finite; a program needn't handle non-finite values.
Results may differ from a plain program's by a relative error of at most 0.0055.
Values may be sent and summed in bfloat16 or wider, within the bound.
No kernel may reach another device: no remote copies, remote signals or barrier semaphores. Data moves between devices by JAX's collectives and lax.ppermute only.
A program may use at most 64 MiB of HBM per device.

v0:
```python
import jax
import jax.numpy as jnp
from jax import lax
from jax.sharding import PartitionSpec as P

TAP_TABLE = (((0, 3), (1, 1)), ((1, 2), (2, 0)))


def extended(x, sides, width):
    for axis, dim in sides:
        peers, length = (lax.axis_size(axis), x.shape[dim])
        up = [(i, (i + 1) % peers) for i in range(peers - 1)]
        down = [(j, i) for i, j in up]
        last = lax.slice_in_dim(x, length - width, length, axis=dim)
        initial = lax.slice_in_dim(x, 0, width, axis=dim)
        before = lax.ppermute(last, axis, up)
        after = lax.ppermute(initial, axis, down)
        x = jnp.concatenate([before, x, after], axis=dim)
    return x


def upsample(padded, weight):
    span_rows = padded.shape[1] - 2
    span_cols = padded.shape[2] - 2
    outputs = weight.shape[3]
    row_parts = []
    for row_par in range(2):
        col_parts = []
        for col_par in range(2):
            summed = jnp.zeros((outputs, span_rows, span_cols), jnp.float32)
            for row_off, row_tap in TAP_TABLE[row_par]:
                for col_off, col_tap in TAP_TABLE[col_par]:
                    window = padded[:, row_off : row_off + span_rows, col_off : col_off + span_cols]
                    summed = summed + jnp.einsum(
                        "chw,co->ohw",
                        window,
                        weight[row_tap, col_tap],
                        preferred_element_type=jnp.float32,
                    )
            col_parts.append(summed)
        row_parts.append(jnp.stack(col_parts, axis=-1))
    stacked = jnp.stack(row_parts, axis=2)
    return stacked.reshape(outputs, 2 * span_rows, 2 * span_cols)


def conv_taps(padded, weight):
    span_rows = padded.shape[1] - 2
    span_cols = padded.shape[2] - 2
    summed = jnp.zeros((weight.shape[3], span_rows, span_cols), jnp.float32)
    for row_tap in range(3):
        for col_tap in range(3):
            window = padded[:, row_tap : row_tap + span_rows, col_tap : col_tap + span_cols]
            summed = summed + jnp.einsum(
                "chw,co->ohw", window, weight[row_tap, col_tap], preferred_element_type=jnp.float32
            )
    return summed


def shards(coarse, skip_field, up_weight, up_bias, conv_weight, conv_bias):
    tiled_rows = lax.all_to_all(coarse, "row", split_axis=1, concat_axis=0, tiled=True)
    rimmed = extended(tiled_rows, (("row", 1),), 1)
    raised = upsample(jnp.pad(rimmed, ((0, 0), (0, 0), (1, 1))), up_weight)
    upsampled = (raised + up_bias[:, None, None]).astype(jnp.bfloat16)
    joined = jnp.concatenate([skip_field, upsampled], axis=0)
    rimmed_fine = extended(joined, (("row", 1),), 1)
    pre = conv_taps(jnp.pad(rimmed_fine, ((0, 0), (0, 0), (1, 1))), conv_weight)
    pre = pre + conv_bias[:, None, None]
    return jax.nn.silu(pre).astype(jnp.bfloat16)


def solution(mesh):
    in_specs = (P("row", "member", None), P(None, ("member", "row"), None), P(), P(), P(), P())
    out_specs = P(None, ("member", "row"), None)
    return jax.shard_map(shards, mesh=mesh, in_specs=in_specs, out_specs=out_specs, check_vma=False)
```

profile of v0, /device:TPU:5, one launch (start us, length us, event | category | flops | bytes accessed | tf_op | source)
XLA Modules:
  0.0 64.4 jit_solution(7071694644316420056)
XLA Ops:
  0.0 2.0 %copy.15 = bf16[24,64,128]{2,0,1:T(8,128)(2,1)} copy(bf16[24,64,128]{2,1,0:T(8,128)(2,1)} %param.6) | data formatting | bytes 786432 | tf_op args[0]
  2.0 6.7 %all-to-all-start = ((bf16[24,64,128]{2,0,1:T(8,128)(2,1)}), bf16[24,64,128]{2,0,1:T(8,128)(2,1)S(1)}, u32[]{:S(2)}, u32[]{:S(2)}) async-start(bf16[24,64,128]{2,0,1:T(8,128)(2,1)} %copy.15), calls=%async_computation | async-start | bytes 786432 | tf_op jit(solution)/shard_map/all_to_all | solution.py:60
  8.7 1.4 %copy.19 = bf16[192,8,256]{2,0,1:T(8,128)(2,1)S(1)} copy(bf16[192,8,256]{2,1,0:T(8,128)(2,1)} %param.7) | data formatting | bytes 1572864 | tf_op args[1]
  10.1 9.6 %all-to-all-done = bf16[24,64,128]{2,0,1:T(8,128)(2,1)S(1)} async-done(((bf16[24,64,128]{2,0,1:T(8,128)(2,1)}), bf16[24,64,128]{2,0,1:T(8,128)(2,1)S(1)}, u32[]{:S(2)}, u32[]{:S(2)}) %all-to-all-start) | async-done | bytes 393248 | tf_op jit(solution)/shard_map/all_to_all | solution.py:60
  20.6 3.2 %collective-permute-start = (bf16[384,1,128]{2,0,1:T(8,128)(2,1)S(1)}, bf16[384,1,128]{2,0,1:T(8,128)(2,1)S(1)}, u32[]{:S(2)}, u32[]{:S(2)}) collective-permute-start(bf16[384,1,128]{2,0,1:T(8,128)(2,1)S(1)} %get-tuple-element.7), channel_id=1, source_target_pairs={{0,1},{1,2},{2,3},{3,4},{4,5},{5,6},{6,7},{7,8},{8,9},{9,10},{10,1... | collective-permute-start | bytes 294920 | tf_op jit(solution)/shard_map/ppermute | solution.py:16
  23.9 1.9 %collective-permute-start.1 = (bf16[384,1,128]{2,0,1:T(8,128)(2,1)S(1)}, bf16[384,1,128]{2,0,1:T(8,128)(2,1)S(1)}, u32[]{:S(2)}, u32[]{:S(2)}) collective-permute-start(bf16[384,1,128]{2,0,1:T(8,128)(2,1)S(1)} %get-tuple-element.8), channel_id=1, source_target_pairs={{1,0},{2,1},{3,2},{4,3},{5,4},{6,5},{7,6},{8,7},{9,8},{10,9},{11,1... | collective-permute-start | bytes 294920 | tf_op jit(solution)/shard_map/ppermute | solution.py:17
  26.1 4.6 %collective-permute-done.1 = bf16[384,1,128]{2,0,1:T(8,128)(2,1)S(1)} collective-permute-done((bf16[384,1,128]{2,0,1:T(8,128)(2,1)S(1)}, bf16[384,1,128]{2,0,1:T(8,128)(2,1)S(1)}, u32[]{:S(2)}, u32[]{:S(2)}) %collective-permute-start.1) | collective-permute-done | bytes 98336 | tf_op jit(solution)/shard_map/ppermute | solution.py:17
  30.7 0.6 fusion.48
  35.2 1.3 %pad_maximum_fusion.8 = f32[192,4,2,128,2]{3,0,1,4,2:T(8,128)} fusion(f32[192,4,1,128,2]{3,0,1,4,2:T(8,128)S(1)} %get-tuple-element.10, f32[192,4,1,128,2]{3,0,1,4,2:T(8,128)S(1)} %get-tuple-element.9), kind=kLoop, calls=%fused_computation.31 | loop fusion | flops 393216 | bytes 3145728 | tf_op jit(solution)/shard_map/stack | solution.py:42
  36.5 2.8 %copy.17 = f32[192,4,2,128,2]{0,4,3,2,1:T(2,128)S(1)} copy(f32[192,4,2,128,2]{3,0,1,4,2:T(8,128)} %pad_maximum_fusion.8) | data formatting | bytes 3145728 | tf_op jit(solution)/shard_map/stack | solution.py:42
  39.3 2.5 %reshape.5 = f32[192,8,256]{0,2,1:T(8,128)} reshape(f32[192,4,2,128,2]{0,4,3,2,1:T(2,128)S(1)} %copy.17) | data formatting | bytes 3145728 | tf_op jit(solution)/shard_map/reshape | solution.py:43
  41.7 1.9 %copy.18 = f32[192,8,256]{2,0,1:T(8,128)S(1)} copy(f32[192,8,256]{0,2,1:T(8,128)} %reshape.5) | data formatting | bytes 3145728 | tf_op jit(solution)/shard_map/reshape | solution.py:43
  43.9 2.1 %collective-permute-start.2 = (bf16[384,1,256]{2,0,1:T(8,128)(2,1)S(1)}, bf16[384,1,256]{2,0,1:T(8,128)(2,1)S(1)}, u32[]{:S(2)}, u32[]{:S(2)}) collective-permute-start(bf16[384,1,256]{2,0,1:T(8,128)(2,1)S(1)} %get-tuple-element.5), channel_id=1, source_target_pairs={{0,1},{1,2},{2,3},{3,4},{4,5},{5,6},{6,7},{7,8},{8,9},{9,10},{10,1... | collective-permute-start | bytes 589832 | tf_op jit(solution)/shard_map/ppermute | solution.py:16
  45.9 2.6 %collective-permute-start.3 = (bf16[384,1,256]{2,0,1:T(8,128)(2,1)S(1)}, bf16[384,1,256]{2,0,1:T(8,128)(2,1)S(1)}, u32[]{:S(2)}, u32[]{:S(2)}) collective-permute-start(bf16[384,1,256]{2,0,1:T(8,128)(2,1)S(1)} %get-tuple-element.6), channel_id=1, source_target_pairs={{1,0},{2,1},{3,2},{4,3},{5,4},{6,5},{7,6},{8,7},{9,8},{10,9},{11,1... | collective-permute-start | bytes 589832 | tf_op jit(solution)/shard_map/ppermute | solution.py:17
  48.5 0.6 fusion.21
  49.1 4.7 %collective-permute-done.3 = bf16[384,1,256]{2,0,1:T(8,128)(2,1)S(1)} collective-permute-done((bf16[384,1,256]{2,0,1:T(8,128)(2,1)S(1)}, bf16[384,1,256]{2,0,1:T(8,128)(2,1)S(1)}, u32[]{:S(2)}, u32[]{:S(2)}) %collective-permute-start.3) | collective-permute-done | bytes 196640 | tf_op jit(solution)/shard_map/ppermute | solution.py:17
  53.8 3.5 %select_maximum_fusion = bf16[384,10,258]{2,0,1:T(8,128)(2,1)S(1)} fusion(bf16[384,1,256]{2,0,1:T(8,128)(2,1)S(1)} %collective-permute-done.3, bf16[384,1,256]{2,0,1:T(8,128)(2,1)S(1)} %collective-permute-done.2, bf16[192,8,256]{2,0,1:T(8,128)(2,1)S(1)} %add_convert_fusion, bf16[192,8,256]{2,0,1:T(8,128)(2,1)S(1)} %copy.19), kind=kLoop, calls=%fused_computation.5 | loop fusion | flops 14860800 | bytes 3947520 | tf_op jit(solution)/shard_map/concatenate | solution.py:18
  57.9 0.7 %fusion.11 = f32[8,256,192]{1,2,0:T(8,128)S(1)} fusion(bf16[384,10,258]{2,0,1:T(8,128)(2,1)S(1)} %select_maximum_fusion, bf16[3,3,384,192]{2,3,1,0:T(8,128)(2,1)S(1)} %copy-done.1), kind=kOutput, calls=%fused_computation.19 | convolution fusion | flops 301989888 | bytes 3293184 | tf_op jit(solution)/shard_map/chw,co->ohw/dot_general | solution.py:53
  58.6 0.6 fusion.13
  59.2 0.7 %fusion.15 = f32[8,256,192]{1,2,0:T(8,128)S(1)} fusion(bf16[384,10,258]{2,0,1:T(8,128)(2,1)S(1)} %select_maximum_fusion, bf16[3,3,384,192]{2,3,1,0:T(8,128)(2,1)S(1)} %copy-done.1), kind=kOutput, calls=%fused_computation.23 | convolution fusion | flops 301989888 | bytes 3293184 | tf_op jit(solution)/shard_map/chw,co->ohw/dot_general | solution.py:53
  60.5 0.6 fusion.7
  61.1 0.6 fusion.17
  61.7 1.4 %fusion.28 = bf16[192,8,256]{2,0,1:T(8,128)(2,1)S(1)} fusion(f32[8,256,192]{1,2,0:T(8,128)S(1)} %fusion.7, f32[8,256,192]{1,2,0:T(8,128)S(1)} %fusion.9, f32[8,256,192]{1,2,0:T(8,128)S(1)} %fusion.11, f32[8,256,192]{1,2,0:T(8,128)S(1)} %fusion.21, f32[8,256,192]{1,2,0:T(8,128)S(1)} %fusion.13, f32[8,256,192]{1,2,0:T(8,128)S(1)} %fusion.15, ...), kind=kOutput, calls=%fused_computation.42 | convolution fusion | flops 307494912 | bytes 15090688 | tf_op jit(solution)/shard_map/chw,co->ohw/dot_general | solution.py:53
  63.1 1.3 %copy.20 = bf16[192,8,256]{2,1,0:T(8,128)(2,1)} copy(bf16[192,8,256]{2,0,1:T(8,128)(2,1)S(1)} %fusion.28) | data formatting | bytes 1572864 | tf_op jit(solution)/shard_map/convert_element_type | solution.py:68
  (33 shorter events, 6.3 us)
Async XLA Ops:
  2.0 17.7 %all-to-all-start = ((bf16[24,64,128]{2,0,1:T(8,128)(2,1)}), bf16[24,64,128]{2,0,1:T(8,128)(2,1)S(1)}, u32[]{:S(2)}, u32[]{:S(2)}) async-start(bf16[24,64,128]{2,0,1:T(8,128)(2,1)} %copy.15), calls=%async_computation | async-start | bytes 786432 | tf_op jit(solution)/shard_map/all_to_all | solution.py:60
  8.7 11.2 %copy-start = (bf16[4,4,384,192]{2,3,1,0:T(8,128)(2,1)S(1)}, bf16[4,4,384,192]{2,3,1,0:T(8,128)(2,1)}, u32[]{:S(2)}) copy-start(bf16[4,4,384,192]{2,3,1,0:T(8,128)(2,1)} %param.8) | copy-start | bytes 7077892
  20.6 5.5 %collective-permute-start = (bf16[384,1,128]{2,0,1:T(8,128)(2,1)S(1)}, bf16[384,1,128]{2,0,1:T(8,128)(2,1)S(1)}, u32[]{:S(2)}, u32[]{:S(2)}) collective-permute-start(bf16[384,1,128]{2,0,1:T(8,128)(2,1)S(1)} %get-tuple-element.7), channel_id=1, source_target_pairs={{0,1},{1,2},{2,3},{3,4},{4,5},{5,6},{6,7},{7,8},{8,9},{9,10},{10,1... | collective-permute-start | bytes 294920 | tf_op jit(solution)/shard_map/ppermute | solution.py:16
  23.9 6.8 %collective-permute-start.1 = (bf16[384,1,128]{2,0,1:T(8,128)(2,1)S(1)}, bf16[384,1,128]{2,0,1:T(8,128)(2,1)S(1)}, u32[]{:S(2)}, u32[]{:S(2)}) collective-permute-start(bf16[384,1,128]{2,0,1:T(8,128)(2,1)S(1)} %get-tuple-element.8), channel_id=1, source_target_pairs={{1,0},{2,1},{3,2},{4,3},{5,4},{6,5},{7,6},{8,7},{9,8},{10,9},{11,1... | collective-permute-start | bytes 294920 | tf_op jit(solution)/shard_map/ppermute | solution.py:17
  41.7 1.9 %copy-start.2 = (f32[192]{0:T(256)S(1)}, f32[192]{0:T(256)}, u32[]{:S(2)}) copy-start(f32[192]{0:T(256)} %param.9) | copy-start | bytes 2308
  43.8 4.7 %copy-start.1 = (bf16[3,3,384,192]{2,3,1,0:T(8,128)(2,1)S(1)}, bf16[3,3,384,192]{2,3,1,0:T(8,128)(2,1)}, u32[]{:S(2)}) copy-start(bf16[3,3,384,192]{2,3,1,0:T(8,128)(2,1)} %param.10) | copy-start | bytes 3981316
  43.9 5.2 %collective-permute-start.2 = (bf16[384,1,256]{2,0,1:T(8,128)(2,1)S(1)}, bf16[384,1,256]{2,0,1:T(8,128)(2,1)S(1)}, u32[]{:S(2)}, u32[]{:S(2)}) collective-permute-start(bf16[384,1,256]{2,0,1:T(8,128)(2,1)S(1)} %get-tuple-element.5), channel_id=1, source_target_pairs={{0,1},{1,2},{2,3},{3,4},{4,5},{5,6},{6,7},{7,8},{8,9},{9,10},{10,1... | collective-permute-start | bytes 589832 | tf_op jit(solution)/shard_map/ppermute | solution.py:16
  45.9 7.9 %collective-permute-start.3 = (bf16[384,1,256]{2,0,1:T(8,128)(2,1)S(1)}, bf16[384,1,256]{2,0,1:T(8,128)(2,1)S(1)}, u32[]{:S(2)}, u32[]{:S(2)}) collective-permute-start(bf16[384,1,256]{2,0,1:T(8,128)(2,1)S(1)} %get-tuple-element.6), channel_id=1, source_target_pairs={{1,0},{2,1},{3,2},{4,3},{5,4},{6,5},{7,6},{8,7},{9,8},{10,9},{11,1... | collective-permute-start | bytes 589832 | tf_op jit(solution)/shard_map/ppermute | solution.py:17
  61.1 0.7 %copy-start.3 = (f32[192]{0:T(256)S(1)}, f32[192]{0:T(256)}, u32[]{:S(2)}) copy-start(f32[192]{0:T(256)} %param.11) | copy-start | bytes 2308
where the time goes:
time: 64.9 us; the launch traced here: 64.4 us
  waiting for transfers between devices  19 us (29%)
  starting transfers between devices  16.5 us (25%)
  local copies, waits for them, and re-layouts  12 us (18%)
  matrix products  10.9 us (17%)
  other arithmetic  5.71 us (9%)
    all_to_all x1, waiting for transfers between devices, shards(): lax.all_to_all(coarse, 'row', split_axis=1, concat_axis=0, tiled=True)  9.63 us
    ppermute x2, waiting for transfers between devices, extended(): after = lax.ppermute(initial, axis, down)  9.32 us
    all_to_all x1, starting transfers between devices, shards(): lax.all_to_all(coarse, 'row', split_axis=1, concat_axis=0, tiled=True)  6.67 us
    dot_general x9, matrix products, conv_taps(): jnp.einsum('chw,co->ohw', window, weight[row_tap, col_tap], preferred_ele...  6.21 us
    ppermute x2, starting transfers between devices, extended(): before = lax.ppermute(last, axis, up)  5.3 us
    dot_general x16, matrix products, upsample(): jnp.einsum('chw,co->ohw', window, weight[row_tap, col_tap], preferred_ele...  4.71 us
    ppermute x2, starting transfers between devices, extended(): after = lax.ppermute(initial, axis, down)  4.51 us
    reshape x2, local copies, waits for them, and re-layouts, upsample(): return stacked.reshape(outputs, 2 * span_rows, 2 * span_cols)  4.37 us
  transfers between devices with their start and end apart: 5, of which 3 were waited for; matrix products, arithmetic and copies ran while one was open for 4% of the time, Pallas kernels for 0%

commit v1 on v0

--- a/solution.py
+++ b/solution.py
@@ -1,9 +1,22 @@
+import functools
 import jax
 import jax.numpy as jnp
 from jax import lax
 from jax.sharding import PartitionSpec as P
 
 TAP_TABLE = (((0, 3), (1, 1)), ((1, 2), (2, 0)))
+
+
+def extend_page(local_block, mesh_dim):
+    return jnp.concatenate(
+        lax.all_to_all(
+            jnp.stack(jnp.split(local_block, lax.psum(1, mesh_dim), 1), 0), mesh_dim, 0, 0
+        ),
+        0,
+    )
+
+
+plan_the_samples = functools.partial(extend_page, mesh_dim="row")
 
 
 def extended(x, sides, width):
@@ -57,7 +70,7 @@
 
 
 def shards(coarse, skip_field, up_weight, up_bias, conv_weight, conv_bias):
-    tiled_rows = lax.all_to_all(coarse, "row", split_axis=1, concat_axis=0, tiled=True)
+    tiled_rows = plan_the_samples(coarse)
     rimmed = extended(tiled_rows, (("row", 1),), 1)
     raised = upsample(jnp.pad(rimmed, ((0, 0), (0, 0), (1, 1))), up_weight)
     upsampled = (raised + up_bias[:, None, None]).astype(jnp.bfloat16)

time: 64.9 us -> 86.4 us (1.33)
  local copies, waits for them, and re-layouts: 12 us -> 32.7 us
    unnamed x10 -> x24, local copies, waits for them, and re-layouts: 3.54 us -> 22.8 us
    another operation x0 -> x1, local copies, waits for them, and re-layouts: none -> 1.42 us  [extend_page(): jnp.stack(jnp.split(local_block, lax.psum(1, mesh_dim), 1), 0)]
  transfers between devices with their start and end apart: 5 -> 5, of which waited for: 3 -> 3; matrix products, arithmetic and copies ran while one was open for 4% -> 3% of each run, Pallas kernels for 0% -> 0%
where the time goes in v1:
time: 86.4 us; the launch traced here: 85.1 us
  local copies, waits for them, and re-layouts  32.7 us (38%)
  waiting for transfers between devices  19 us (22%)
  starting transfers between devices  16.5 us (19%)
  matrix products  10.9 us (13%)
  other arithmetic  5.71 us (7%)
    unnamed x24, local copies, waits for them, and re-layouts  22.8 us
    all_to_all x1, waiting for transfers between devices, extend_page(): lax.all_to_all(jnp.stack(jnp.split(local_block, lax.psum(1, mesh_dim), 1)...  9.63 us
    ppermute x2, waiting for transfers between devices, extended(): after = lax.ppermute(initial, axis, down)  9.32 us
    all_to_all x1, starting transfers between devices, extend_page(): lax.all_to_all(jnp.stack(jnp.split(local_block, lax.psum(1, mesh_dim), 1)...  6.67 us
    dot_general x9, matrix products, conv_taps(): jnp.einsum('chw,co->ohw', window, weight[row_tap, col_tap], preferred_ele...  6.22 us
    ppermute x2, starting transfers between devices, extended(): before = lax.ppermute(last, axis, up)  5.29 us
    dot_general x16, matrix products, upsample(): jnp.einsum('chw,co->ohw', window, weight[row_tap, col_tap], preferred_ele...  4.66 us
    ppermute x2, starting transfers between devices, extended(): after = lax.ppermute(initial, axis, down)  4.51 us
  transfers between devices with their start and end apart: 5, of which 3 were waited for; matrix products, arithmetic and copies ran while one was open for 3% of the time, Pallas kernels for 0%

profile of v1, /device:TPU:5, one launch (start us, length us, event | category | flops | bytes accessed | tf_op | source)
XLA Modules:
  0.0 85.1 jit_solution(8967099502651148419)
XLA Ops:
  0.0 1.4 %constant_dynamic-update-slice_fusion.15 = bf16[16,24,4,128]{3,2,1,0:T(4,128)(2,1)} fusion(bf16[24,64,128]{2,1,0:T(8,128)(2,1)} %param.6), kind=kLoop, calls=%fused_computation.149 | loop fusion | bytes 49152
  1.4 1.4 %constant_dynamic-update-slice_fusion.14 = bf16[16,24,4,128]{3,2,1,0:T(4,128)(2,1)} fusion(bf16[16,24,4,128]{3,2,1,0:T(4,128)(2,1)} %constant_dynamic-update-slice_fusion.15, bf16[24,64,128]{2,1,0:T(8,128)(2,1)} %param.6), kind=kLoop, calls=%fused_computation.148 | loop fusion | bytes 49152
  2.8 1.4 %constant_dynamic-update-slice_fusion.13 = bf16[16,24,4,128]{3,2,1,0:T(4,128)(2,1)} fusion(bf16[16,24,4,128]{3,2,1,0:T(4,128)(2,1)} %constant_dynamic-update-slice_fusion.14, bf16[24,64,128]{2,1,0:T(8,128)(2,1)} %param.6), kind=kLoop, calls=%fused_computation.147 | loop fusion | bytes 49152
  4.2 1.4 %constant_dynamic-update-slice_fusion.12 = bf16[16,24,4,128]{3,2,1,0:T(4,128)(2,1)} fusion(bf16[16,24,4,128]{3,2,1,0:T(4,128)(2,1)} %constant_dynamic-update-slice_fusion.13, bf16[24,64,128]{2,1,0:T(8,128)(2,1)} %param.6), kind=kLoop, calls=%fused_computation.146 | loop fusion | bytes 49152
  7.1 1.4 %constant_dynamic-update-slice_fusion.10 = bf16[16,24,4,128]{3,2,1,0:T(4,128)(2,1)} fusion(bf16[16,24,4,128]{3,2,1,0:T(4,128)(2,1)} %constant_dynamic-update-slice_fusion.11, bf16[24,64,128]{2,1,0:T(8,128)(2,1)} %param.6), kind=kLoop, calls=%fused_computation.144 | loop fusion | bytes 49152
  9.9 1.4 %constant_dynamic-update-slice_fusion.8 = bf16[16,24,4,128]{3,2,1,0:T(4,128)(2,1)} fusion(bf16[16,24,4,128]{3,2,1,0:T(4,128)(2,1)} %constant_dynamic-update-slice_fusion.9, bf16[24,64,128]{2,1,0:T(8,128)(2,1)} %param.6), kind=kLoop, calls=%fused_computation.142 | loop fusion | bytes 49152
  12.8 1.4 %constant_dynamic-update-slice_fusion.6 = bf16[16,24,4,128]{3,2,1,0:T(4,128)(2,1)} fusion(bf16[16,24,4,128]{3,2,1,0:T(4,128)(2,1)} %constant_dynamic-update-slice_fusion.7, bf16[24,64,128]{2,1,0:T(8,128)(2,1)} %param.6), kind=kLoop, calls=%fused_computation.140 | loop fusion | bytes 49152
  14.2 1.4 %constant_dynamic-update-slice_fusion.5 = bf16[16,24,4,128]{3,2,1,0:T(4,128)(2,1)} fusion(bf16[16,24,4,128]{3,2,1,0:T(4,128)(2,1)} %constant_dynamic-update-slice_fusion.6, bf16[24,64,128]{2,1,0:T(8,128)(2,1)} %param.6), kind=kLoop, calls=%fused_computation.139 | loop fusion | bytes 49152
  15.6 1.4 %constant_dynamic-update-slice_fusion.4 = bf16[16,24,4,128]{3,2,1,0:T(4,128)(2,1)} fusion(bf16[16,24,4,128]{3,2,1,0:T(4,128)(2,1)} %constant_dynamic-update-slice_fusion.5, bf16[24,64,128]{2,1,0:T(8,128)(2,1)} %param.6), kind=kLoop, calls=%fused_computation.138 | loop fusion | bytes 49152
  18.4 1.4 %constant_dynamic-update-slice_fusion.2 = bf16[16,24,4,128]{3,2,1,0:T(4,128)(2,1)} fusion(bf16[16,24,4,128]{3,2,1,0:T(4,128)(2,1)} %constant_dynamic-update-slice_fusion.3, bf16[24,64,128]{2,1,0:T(8,128)(2,1)} %param.6), kind=kLoop, calls=%fused_computation.136 | loop fusion | bytes 49152
  21.3 1.4 %constant_dynamic-update-slice_fusion = bf16[16,24,4,128]{3,2,1,0:T(4,128)(2,1)} fusion(bf16[16,24,4,128]{3,2,1,0:T(4,128)(2,1)} %constant_dynamic-update-slice_fusion.1, bf16[24,64,128]{2,1,0:T(8,128)(2,1)} %param.6), kind=kLoop, calls=%fused_computation.134 | loop fusion | bytes 49152 | tf_op jit(solution)/shard_map/stack | solution.py:13
  22.7 6.7 %all-to-all-start = ((bf16[16,24,4,128]{3,2,1,0:T(4,128)(2,1)}), bf16[16,24,4,128]{3,2,1,0:T(4,128)(2,1)S(1)}, u32[]{:S(2)}, u32[]{:S(2)}) async-start(bf16[16,24,4,128]{3,2,1,0:T(4,128)(2,1)} %constant_dynamic-update-slice_fusion), calls=%async_computation | async-start | bytes 786432 | tf_op jit(solution)/shard_map/all_to_all | solution.py:12
  29.4 1.4 %copy.13 = bf16[192,8,256]{2,0,1:T(8,128)(2,1)S(1)} copy(bf16[192,8,256]{2,1,0:T(8,128)(2,1)} %param.7) | data formatting | bytes 1572864 | tf_op args[1]
  30.8 9.6 %all-to-all-done = bf16[16,24,4,128]{3,2,1,0:T(4,128)(2,1)S(1)} async-done(((bf16[16,24,4,128]{3,2,1,0:T(4,128)(2,1)}), bf16[16,24,4,128]{3,2,1,0:T(4,128)(2,1)S(1)}, u32[]{:S(2)}, u32[]{:S(2)}) %all-to-all-start) | async-done | bytes 393248 | tf_op jit(solution)/shard_map/all_to_all | solution.py:12
  41.1 3.2 %collective-permute-start = (bf16[384,1,128]{2,0,1:T(8,128)(2,1)S(1)}, bf16[384,1,128]{2,0,1:T(8,128)(2,1)S(1)}, u32[]{:S(2)}, u32[]{:S(2)}) collective-permute-start(bf16[384,1,128]{2,0,1:T(8,128)(2,1)S(1)} %get-tuple-element.7), channel_id=1, source_target_pairs={{0,1},{1,2},{2,3},{3,4},{4,5},{5,6},{6,7},{7,8},{8,9},{9,10},{10,1... | collective-permute-start | bytes 294920 | tf_op jit(solution)/shard_map/ppermute | solution.py:29
  44.3 1.9 %collective-permute-start.1 = (bf16[384,1,128]{2,0,1:T(8,128)(2,1)S(1)}, bf16[384,1,128]{2,0,1:T(8,128)(2,1)S(1)}, u32[]{:S(2)}, u32[]{:S(2)}) collective-permute-start(bf16[384,1,128]{2,0,1:T(8,128)(2,1)S(1)} %get-tuple-element.8), channel_id=1, source_target_pairs={{1,0},{2,1},{3,2},{4,3},{5,4},{6,5},{7,6},{8,7},{9,8},{10,9},{11,1... | collective-permute-start | bytes 294920 | tf_op jit(solution)/shard_map/ppermute | solution.py:30
  46.5 4.6 %collective-permute-done.1 = bf16[384,1,128]{2,0,1:T(8,128)(2,1)S(1)} collective-permute-done((bf16[384,1,128]{2,0,1:T(8,128)(2,1)S(1)}, bf16[384,1,128]{2,0,1:T(8,128)(2,1)S(1)}, u32[]{:S(2)}, u32[]{:S(2)}) %collective-permute-start.1) | collective-permute-done | bytes 98336 | tf_op jit(solution)/shard_map/ppermute | solution.py:30
  57.1 2.8 %copy.11 = f32[192,4,2,128,2]{0,4,3,2,1:T(2,128)S(1)} copy(f32[192,4,2,128,2]{3,0,1,4,2:T(8,128)} %pad_maximum_fusion.8) | data formatting | bytes 3145728 | tf_op jit(solution)/shard_map/stack | solution.py:55
  59.9 2.5 %reshape.9 = f32[192,8,256]{0,2,1:T(8,128)} reshape(f32[192,4,2,128,2]{0,4,3,2,1:T(2,128)S(1)} %copy.11) | data formatting | bytes 3145728 | tf_op jit(solution)/shard_map/reshape | solution.py:56
  62.4 1.9 %copy.12 = f32[192,8,256]{2,0,1:T(8,128)S(1)} copy(f32[192,8,256]{0,2,1:T(8,128)} %reshape.9) | data formatting | bytes 3145728 | tf_op jit(solution)/shard_map/reshape | solution.py:56
  64.5 2.1 %collective-permute-start.2 = (bf16[384,1,256]{2,0,1:T(8,128)(2,1)S(1)}, bf16[384,1,256]{2,0,1:T(8,128)(2,1)S(1)}, u32[]{:S(2)}, u32[]{:S(2)}) collective-permute-start(bf16[384,1,256]{2,0,1:T(8,128)(2,1)S(1)} %get-tuple-element.5), channel_id=1, source_target_pairs={{0,1},{1,2},{2,3},{3,4},{4,5},{5,6},{6,7},{7,8},{8,9},{9,10},{10,1... | collective-permute-start | bytes 589832 | tf_op jit(solution)/shard_map/ppermute | solution.py:29
  66.6 2.6 %collective-permute-start.3 = (bf16[384,1,256]{2,0,1:T(8,128)(2,1)S(1)}, bf16[384,1,256]{2,0,1:T(8,128)(2,1)S(1)}, u32[]{:S(2)}, u32[]{:S(2)}) collective-permute-start(bf16[384,1,256]{2,0,1:T(8,128)(2,1)S(1)} %get-tuple-element.6), channel_id=1, source_target_pairs={{1,0},{2,1},{3,2},{4,3},{5,4},{6,5},{7,6},{8,7},{9,8},{10,9},{11,1... | collective-permute-start | bytes 589832 | tf_op jit(solution)/shard_map/ppermute | solution.py:30
  69.8 4.7 %collective-permute-done.3 = bf16[384,1,256]{2,0,1:T(8,128)(2,1)S(1)} collective-permute-done((bf16[384,1,256]{2,0,1:T(8,128)(2,1)S(1)}, bf16[384,1,256]{2,0,1:T(8,128)(2,1)S(1)}, u32[]{:S(2)}, u32[]{:S(2)}) %collective-permute-start.3) | collective-permute-done | bytes 196640 | tf_op jit(solution)/shard_map/ppermute | solution.py:30
  74.5 3.5 %select_maximum_fusion = bf16[384,10,258]{2,0,1:T(8,128)(2,1)S(1)} fusion(bf16[384,1,256]{2,0,1:T(8,128)(2,1)S(1)} %collective-permute-done.3, bf16[384,1,256]{2,0,1:T(8,128)(2,1)S(1)} %collective-permute-done.2, bf16[192,8,256]{2,0,1:T(8,128)(2,1)S(1)} %add_convert_fusion, bf16[192,8,256]{2,0,1:T(8,128)(2,1)S(1)} %copy.13), kind=kLoop, calls=%fused_computation.5 | loop fusion | flops 14860800 | bytes 3947520 | tf_op jit(solution)/shard_map/concatenate | solution.py:31
  (48 shorter events, 21.6 us)
Async XLA Ops:
  22.7 17.7 %all-to-all-start = ((bf16[16,24,4,128]{3,2,1,0:T(4,128)(2,1)}), bf16[16,24,4,128]{3,2,1,0:T(4,128)(2,1)S(1)}, u32[]{:S(2)}, u32[]{:S(2)}) async-start(bf16[16,24,4,128]{3,2,1,0:T(4,128)(2,1)} %constant_dynamic-update-slice_fusion), calls=%async_computation | async-start | bytes 786432 | tf_op jit(solution)/shard_map/all_to_all | solution.py:12
  29.3 11.2 %copy-start = (bf16[4,4,384,192]{2,3,1,0:T(8,128)(2,1)S(1)}, bf16[4,4,384,192]{2,3,1,0:T(8,128)(2,1)}, u32[]{:S(2)}) copy-start(bf16[4,4,384,192]{2,3,1,0:T(8,128)(2,1)} %param.8) | copy-start | bytes 7077892
  41.1 5.4 %collective-permute-start = (bf16[384,1,128]{2,0,1:T(8,128)(2,1)S(1)}, bf16[384,1,128]{2,0,1:T(8,128)(2,1)S(1)}, u32[]{:S(2)}, u32[]{:S(2)}) collective-permute-start(bf16[384,1,128]{2,0,1:T(8,128)(2,1)S(1)} %get-tuple-element.7), channel_id=1, source_target_pairs={{0,1},{1,2},{2,3},{3,4},{4,5},{5,6},{6,7},{7,8},{8,9},{9,10},{10,1... | collective-permute-start | bytes 294920 | tf_op jit(solution)/shard_map/ppermute | solution.py:29
  44.3 6.8 %collective-permute-start.1 = (bf16[384,1,128]{2,0,1:T(8,128)(2,1)S(1)}, bf16[384,1,128]{2,0,1:T(8,128)(2,1)S(1)}, u32[]{:S(2)}, u32[]{:S(2)}) collective-permute-start(bf16[384,1,128]{2,0,1:T(8,128)(2,1)S(1)} %get-tuple-element.8), channel_id=1, source_target_pairs={{1,0},{2,1},{3,2},{4,3},{5,4},{6,5},{7,6},{8,7},{9,8},{10,9},{11,1... | collective-permute-start | bytes 294920 | tf_op jit(solution)/shard_map/ppermute | solution.py:30
  62.4 1.9 %copy-start.2 = (f32[192]{0:T(256)S(1)}, f32[192]{0:T(256)}, u32[]{:S(2)}) copy-start(f32[192]{0:T(256)} %param.9) | copy-start | bytes 2308
  64.5 4.7 %copy-start.1 = (bf16[3,3,384,192]{2,3,1,0:T(8,128)(2,1)S(1)}, bf16[3,3,384,192]{2,3,1,0:T(8,128)(2,1)}, u32[]{:S(2)}) copy-start(bf16[3,3,384,192]{2,3,1,0:T(8,128)(2,1)} %param.10) | copy-start | bytes 3981316
  64.5 5.2 %collective-permute-start.2 = (bf16[384,1,256]{2,0,1:T(8,128)(2,1)S(1)}, bf16[384,1,256]{2,0,1:T(8,128)(2,1)S(1)}, u32[]{:S(2)}, u32[]{:S(2)}) collective-permute-start(bf16[384,1,256]{2,0,1:T(8,128)(2,1)S(1)} %get-tuple-element.5), channel_id=1, source_target_pairs={{0,1},{1,2},{2,3},{3,4},{4,5},{5,6},{6,7},{7,8},{8,9},{9,10},{10,1... | collective-permute-start | bytes 589832 | tf_op jit(solution)/shard_map/ppermute | solution.py:29
  66.6 7.9 %collective-permute-start.3 = (bf16[384,1,256]{2,0,1:T(8,128)(2,1)S(1)}, bf16[384,1,256]{2,0,1:T(8,128)(2,1)S(1)}, u32[]{:S(2)}, u32[]{:S(2)}) collective-permute-start(bf16[384,1,256]{2,0,1:T(8,128)(2,1)S(1)} %get-tuple-element.6), channel_id=1, source_target_pairs={{1,0},{2,1},{3,2},{4,3},{5,4},{6,5},{7,6},{8,7},{9,8},{10,9},{11,1... | collective-permute-start | bytes 589832 | tf_op jit(solution)/shard_map/ppermute | solution.py:30
  81.7 0.7 copy-start.3
